TPU v7x, 256 devices: a whole 4x4x8 slice. The times are simulated.
256 devices in a mesh: row: 16 (over y, x_lo, core), col: 16 (over x_hi, z).
Axes of the slice: x: 4 (x_hi: 2, x_lo: 2; x = x_hi * 2 + x_lo), y: 4, z: 8, core: 2. Of those that a mesh axis runs over, the one named last changes fastest.
Arguments:
- stored_blocks: float32 [512, 16, 128, 128], P('row', 'col'), may hold values from -1.8 to 1.8
- block_cols: int32 [512, 16], P('row', 'col'), may hold values from 0 to 31, as said below
- storage_map: int32 [512, 16], P('row', 'col'), may hold values from 0 to 1, as said below
Outputs:
- square_part: float32 [512, 16, 128, 128], P('row', 'col')
Inputs may be any that keep to these rules, and one draw needn't show every extreme that they name: The block pattern is symmetric: block (R, q) with column C = q * 32 + block_cols[R, q] has block_cols[C, R // 32] == R mod 32; every slab pairs its block rows with its block columns one to one; block_cols[R, R // 32] == R mod 32. Of a block and its mirror image exactly one has storage_map 1; blocks on the diagonal have 1.
All inputs are finite; a program needn't handle non-finite values.
Results may differ from a plain program's by a relative error of at most 0.0001.
Values sent between devices are 32-bit elements; how exact they have to be, the bound alone decides.
No kernel may reach another device: no remote copies, remote signals or barrier semaphores. Data moves between devices by JAX's collectives and lax.ppermute only.
A program may use at most 128 MiB of HBM per device.

v0:
```python
import jax
import jax.numpy as jnp
from jax import lax
from jax.sharding import PartitionSpec as P

STEPS = 4


def shifted(block, axis, distance):
    size = lax.axis_size(axis)
    route = [((i + distance) % size, i) for i in range(size)]
    return lax.ppermute(block, axis, route)


def transposed(block, rows, cols):
    route = [(b * cols + a, a * cols + b) for a in range(rows) for b in range(cols)]
    return lax.ppermute(block, ("row", "col"), route)


def shards(stored_blocks, block_cols, storage_map):
    rows = lax.axis_size("row")
    cols = lax.axis_size("col")
    local_rows = stored_blocks.shape[0]
    bs = stored_blocks.shape[-1]
    row_index = lax.axis_index("row")
    col_index = lax.axis_index("col")
    row_cols = lax.all_gather(block_cols, "col", axis=1, tiled=True)
    col_cols = lax.all_gather(block_cols, "row", axis=0, tiled=True)[:, 0]
    held = stored_blocks[:, 0] * storage_map.astype(jnp.float32)[:, :, None]
    arrived = transposed(held, rows, cols)
    density = held + jnp.swapaxes(arrived[block_cols[:, 0]], 1, 2)
    inverse = (
        jnp.zeros((local_rows,), jnp.int32)
        .at[block_cols[:, 0]]
        .set(jnp.arange(local_rows, dtype=jnp.int32))
    )
    mirror_out = jnp.swapaxes(held[inverse], 1, 2)
    chunk = local_rows // cols
    pieces = jnp.stack([held, mirror_out]).reshape(2, cols, chunk, bs, bs)
    spread = lax.all_to_all(pieces, "col", 1, 1, tiled=True)
    mine = []
    for step in range(STEPS):
        own = lax.dynamic_index_in_dim(spread[0], (row_index + step) % cols, 0, keepdims=False)
        far = lax.dynamic_index_in_dim(spread[1], (row_index - step) % cols, 0, keepdims=False)
        if step:
            far = shifted(far, "row", step)
        mine.append(own + far)
    mine = jnp.stack(mine)
    left_all = lax.all_gather(mine, "col", axis=0, tiled=False)
    left_all = jnp.transpose(left_all, (1, 0, 2, 3, 4)).reshape(STEPS, local_rows, bs, bs)
    one = shifted(density, "row", 1)
    two = shifted(density, "row", 2)
    three = shifted(two, "row", 1)
    rights = [density, one, two, three]
    own_cols = block_cols[:, 0]
    total = jnp.zeros(density.shape, jnp.float32)
    for step in range(STEPS):
        kappa = (row_index + step) % cols
        inner = lax.dynamic_index_in_dim(row_cols, kappa, 1, keepdims=False)
        right = rights[step][inner]
        panel_cols = lax.dynamic_slice_in_dim(col_cols, kappa * local_rows, local_rows)
        match = panel_cols[inner] == own_cols
        term = jnp.einsum("rik,rkj->rij", left_all[step], right, precision=lax.Precision.HIGHEST)
        total = total + jnp.where(match[:, None, None], term, jnp.float32(0.0))
    return total[:, None]


def solution(mesh):
    return jax.shard_map(
        shards,
        mesh=mesh,
        in_specs=(P("row", "col", None, None), P("row", "col"), P("row", "col")),
        out_specs=P("row", "col", None, None),
        check_vma=False,
    )
```

profile of v0, /device:TPU:2, one launch (start us, length us, event | category | flops | bytes accessed | tf_op | source)
XLA Modules:
  0.0 501.1 jit_solution(3726696630393694125)
XLA Ops:
  6.5 0.7 convert_bitcast_fusion
  7.2 0.7 convert_reduce_fusion
  7.9 0.0 copy-start.5
  7.9 1.9 copy.13
  9.8 0.0 copy-done.5
  9.8 0.7 scatter_custom_fusion
  10.5 0.1 mul.37
  10.6 1.5 bitcast_multiply_fusion
  12.2 3.6 gather_fusion.1
  15.8 1.9 broadcast_multiply_fusion
  17.7 0.3 copy-done.3
  18.0 2.3 pad_maximum_fusion
  20.2 10.2 %all-to-all-start = ((f32[2,16,2,128,128]{4,3,2,0,1:T(8,128)}), f32[2,16,2,128,128]{4,3,2,0,1:T(8,128)}, u32[]{:S(2)}, u32[]{:S(2)}) async-start(f32[2,16,2,128,128]{4,3,2,0,1:T(8,128)} %pad_maximum_fusion), calls=%async_computation | async-start | bytes 8388608 | tf_op jit(solution)/shard_map/all_to_all | solution.py:40
  30.4 0.0 all-gather.4.cloned.1.call-start
  30.6 96.6 %all-to-all-done = f32[2,16,2,128,128]{4,3,2,0,1:T(8,128)} async-done(((f32[2,16,2,128,128]{4,3,2,0,1:T(8,128)}), f32[2,16,2,128,128]{4,3,2,0,1:T(8,128)}, u32[]{:S(2)}, u32[]{:S(2)}) %all-to-all-start) | async-done | bytes 4194336 | tf_op jit(solution)/shard_map/all_to_all | solution.py:40
  127.1 2.5 fusion.15
  129.6 0.0 copy-start.4
  129.7 1.3 copy-done.4
  131.0 0.2 collective-permute-start
  131.3 3.0 collective-permute-start.1
  134.3 1.1 collective-permute-start.2
  135.4 0.0 collective-permute-done
  135.4 5.2 %collective-permute-done.1 = f32[2,128,128]{2,1,0:T(8,128)S(1)} collective-permute-done((f32[2,128,128]{2,1,0:T(8,128)S(1)}, f32[2,128,128]{2,1,0:T(8,128)S(1)}, u32[]{:S(2)}, u32[]{:S(2)}) %collective-permute-start.1) | collective-permute-done | bytes 131104 | tf_op jit(solution)/shard_map/ppermute | solution.py:12
  140.6 1.3 collective-permute-done.2
  141.8 1.1 fusion.2
  142.9 0.9 pad_maximum_fusion.1
  143.8 0.0 all-gather.4.cloned.1.call-update
  143.8 1.9 collective-permute-start.3
  145.7 158.7 %collective-permute-done.3 = f32[32,128,128]{1,2,0:T(8,128)} collective-permute-done((f32[32,128,128]{1,2,0:T(8,128)}, f32[32,128,128]{1,2,0:T(8,128)}, u32[]{:S(2)}, u32[]{:S(2)}) %collective-permute-start.3) | collective-permute-done | bytes 2097184 | tf_op jit(solution)/shard_map/ppermute | solution.py:17
  304.5 3.1 copy.15
  307.5 3.7 gather_fusion.2
  311.2 0.0 copy-start.6
  311.2 3.2 bitcast_add_fusion
  314.4 0.0 collective-permute-start.5
  314.4 6.1 %collective-permute-start.4 = (f32[32,128,128]{1,2,0:T(8,128)}, f32[32,128,128]{1,2,0:T(8,128)}, u32[]{:S(2)}, u32[]{:S(2)}) collective-permute-start(f32[32,128,128]{1,2,0:T(8,128)} %bitcast_add_fusion), channel_id=1, source_target_pairs={{16,0},{32,16},{48,32},{64,48},{80,64},{96,80},{112,96},{128,112},... | collective-permute-start | bytes 6291464 | tf_op jit(solution)/shard_map/ppermute | solution.py:12
  320.5 60.3 %collective-permute-done.5 = f32[32,128,128]{1,2,0:T(8,128)} collective-permute-done((f32[32,128,128]{1,2,0:T(8,128)}, f32[32,128,128]{1,2,0:T(8,128)}, u32[]{:S(2)}, u32[]{:S(2)}) %collective-permute-start.5) | collective-permute-done | bytes 2097184 | tf_op jit(solution)/shard_map/ppermute | solution.py:12
  380.8 14.7 %collective-permute-start.6 = (f32[32,128,128]{1,2,0:T(8,128)}, f32[32,128,128]{1,2,0:T(8,128)}, u32[]{:S(2)}, u32[]{:S(2)}) collective-permute-start(f32[32,128,128]{1,2,0:T(8,128)} %collective-permute-done.5), channel_id=1, source_target_pairs={{16,0},{32,16},{48,32},{64,48},{80,64},{96,80},{112,96},{128,112},... | collective-permute-start | bytes 6291464 | tf_op jit(solution)/shard_map/ppermute | solution.py:12
  395.4 0.0 copy-done.6
  395.4 0.7 dynamic-slice.12
  396.8 42.1 %all-gather.1 = s32[16,1,32]{2,1,0:T(1,128)S(1)} all-gather(s32[1,1,32]{2,1,0:T(1,128)S(1)} %bitcast.100), channel_id=1, replica_groups=mesh['row'=16,'col'=16] {'col'}, dimensions={0}, use_global_device_ids=true | all-gather | bytes 2176 | tf_op jit(solution)/shard_map/all_gather | solution.py:27
  438.9 0.1 bitcast_dynamic-update-slice_fusion
  439.0 15.4 %all-reduce = s32[512]{0:T(512)S(1)} all-reduce(s32[512]{0:T(512)S(1)} %bitcast_dynamic-update-slice_fusion), channel_id=1, replica_groups=mesh['row'=16,'col'=16] {'row'}, use_global_device_ids=true, to_apply=%add | all-reduce | flops 512 | bytes 4096
  454.4 0.1 fusion.16
  454.5 0.7 gather_fusion
  455.2 0.7 gather_fusion.4
  455.9 0.7 gather_fusion.6
  456.6 0.7 gather_fusion.8
  457.3 3.6 gather_fusion.3
  460.9 2.3 gather_fusion.7
  463.2 0.0 collective-permute-done.4
  463.2 3.6 gather_fusion.5
  466.8 0.0 collective-permute-done.6
  466.8 3.7 gather_fusion.9
  470.4 0.0 all-gather.4.cloned.1.call-done
  470.4 0.0 copy-start.1
  470.4 4.2 fusion.14
  474.6 0.0 copy-done.1
  474.7 0.0 copy-start
  474.7 4.5 fusion.18
  479.2 0.0 copy-done
  479.2 4.5 fusion.17
  483.7 4.5 fusion.19
  488.2 0.0 copy-done.2
  488.2 6.0 %add_bitcast_fusion = f32[32,1,128,128]{3,2,1,0:T(8,128)} fusion(f32[32,128,128]{2,1,0:T(8,128)S(1)} %fusion.19, f32[32,128,128]{2,1,0:T(8,128)S(1)} %fusion.18, f32[32,128,128]{2,1,0:T(8,128)S(1)} %fusion.17, f32[32,128,128]{2,1,0:T(8,128)S(1)} %bitcast.99, f32[32,128,128]{1,2,0:T(8,128)S(1)} %copy-done.2, pred[32]{0:T(512)(128)(4,1)S(1)} %get-tuple-element.29, ...), kind=kOutput, calls=%fused_computation.14 | convolution fusion | flops 808976384 | bytes 12583040 | tf_op jit(solution)/shard_map/rik,rkj->rij/dot_general | solution.py:63
  (15 shorter events, 0.1 us)
Async XLA Ops:
  7.9 1.9 copy-start.5
  15.8 2.2 copy-start.3
  20.2 106.9 %all-to-all-start = ((f32[2,16,2,128,128]{4,3,2,0,1:T(8,128)}), f32[2,16,2,128,128]{4,3,2,0,1:T(8,128)}, u32[]{:S(2)}, u32[]{:S(2)}) async-start(f32[2,16,2,128,128]{4,3,2,0,1:T(8,128)} %pad_maximum_fusion), calls=%async_computation | async-start | bytes 8388608 | tf_op jit(solution)/shard_map/all_to_all | solution.py:40
  30.4 440.0 %all-gather.4.cloned.1.call-start = ((), (), s32[]{:S(2)}) async-start(), calls=%async_computation.1 | async-start | bytes 8912896 | tf_op jit(solution)/shard_map/all_gather | solution.py:49
  129.6 1.3 copy-start.4
  131.0 4.4 collective-permute-start
  131.3 9.3 %collective-permute-start.1 = (f32[2,128,128]{2,1,0:T(8,128)S(1)}, f32[2,128,128]{2,1,0:T(8,128)S(1)}, u32[]{:S(2)}, u32[]{:S(2)}) collective-permute-start(f32[2,128,128]{2,1,0:T(8,128)S(1)} %get-tuple-element.13), channel_id=1, source_target_pairs={{32,0},{48,16},{64,32},{80,48},{96,64},{112,80},{128,96},{144,112}... | collective-permute-start | bytes 393224 | tf_op jit(solution)/shard_map/ppermute | solution.py:12
  134.3 7.5 %collective-permute-start.2 = (f32[2,128,128]{2,1,0:T(8,128)S(1)}, f32[2,128,128]{2,1,0:T(8,128)S(1)}, u32[]{:S(2)}, u32[]{:S(2)}) collective-permute-start(f32[2,128,128]{2,1,0:T(8,128)S(1)} %get-tuple-element.12), channel_id=1, source_target_pairs={{48,0},{64,16},{80,32},{96,48},{112,64},{128,80},{144,96},{160,112... | collective-permute-start | bytes 393224 | tf_op jit(solution)/shard_map/ppermute | solution.py:12
  143.8 160.7 %collective-permute-start.3 = (f32[32,128,128]{1,2,0:T(8,128)}, f32[32,128,128]{1,2,0:T(8,128)}, u32[]{:S(2)}, u32[]{:S(2)}) collective-permute-start(f32[32,128,128]{1,2,0:T(8,128)} %bitcast_multiply_fusion), channel_id=1, source_target_pairs={{0,0},{16,1},{32,2},{48,3},{64,4},{80,5},{96,6},{112,7},{128,8},{1... | collective-permute-start | bytes 6291464 | tf_op jit(solution)/shard_map/ppermute | solution.py:17
  311.2 84.3 %copy-start.6 = (u32[256]{0:T(256)S(1)}, u32[256]{0:T(256)}, u32[]{:S(2)}) copy-start(u32[256]{0:T(256)} %constant.118) | copy-start | bytes 3076
  314.4 66.4 %collective-permute-start.5 = (f32[32,128,128]{1,2,0:T(8,128)}, f32[32,128,128]{1,2,0:T(8,128)}, u32[]{:S(2)}, u32[]{:S(2)}) collective-permute-start(f32[32,128,128]{1,2,0:T(8,128)} %bitcast_add_fusion), channel_id=1, source_target_pairs={{32,0},{48,16},{64,32},{80,48},{96,64},{112,80},{128,96},{144,112}... | collective-permute-start | bytes 6291464 | tf_op jit(solution)/shard_map/ppermute | solution.py:12
  314.4 148.8 %collective-permute-start.4 = (f32[32,128,128]{1,2,0:T(8,128)}, f32[32,128,128]{1,2,0:T(8,128)}, u32[]{:S(2)}, u32[]{:S(2)}) collective-permute-start(f32[32,128,128]{1,2,0:T(8,128)} %bitcast_add_fusion), channel_id=1, source_target_pairs={{16,0},{32,16},{48,32},{64,48},{80,64},{96,80},{112,96},{128,112},... | collective-permute-start | bytes 6291464 | tf_op jit(solution)/shard_map/ppermute | solution.py:12
  380.8 86.0 %collective-permute-start.6 = (f32[32,128,128]{1,2,0:T(8,128)}, f32[32,128,128]{1,2,0:T(8,128)}, u32[]{:S(2)}, u32[]{:S(2)}) collective-permute-start(f32[32,128,128]{1,2,0:T(8,128)} %collective-permute-done.5), channel_id=1, source_target_pairs={{16,0},{32,16},{48,32},{64,48},{80,64},{96,80},{112,96},{128,112},... | collective-permute-start | bytes 6291464 | tf_op jit(solution)/shard_map/ppermute | solution.py:12
  470.4 4.2 copy-start.1
  474.7 4.5 copy-start
  483.7 4.5 copy-start.2
Sparse Core Ops, SparseCore 0:
  143.9 279.5 all-gather.3
where the time goes:
time: 503 us; the launch traced here: 501 us
  waiting for transfers between devices  322 us (64%)
  blocking collectives  57.5 us (11%)
  local copies, waits for them, and re-layouts  38.1 us (8%)
  starting transfers between devices  37.3 us (7%)
  matrix products  19.5 us (4%)
  between operations  14.4 us (3%)
  other arithmetic  12.3 us (2%)
    ppermute x1, waiting for transfers between devices, transposed(): return lax.ppermute(block, ('row', 'col'), route)  159 us
    all_to_all x1, waiting for transfers between devices, shards(): spread = lax.all_to_all(pieces, 'col', 1, 1, tiled=True)  96.6 us
    ppermute x6, waiting for transfers between devices, shifted(): return lax.ppermute(block, axis, route)  66.8 us
    all_gather x1, blocking collectives, shards(): row_cols = lax.all_gather(block_cols, 'col', axis=1, tiled=True)  42.1 us
    ppermute x6, starting transfers between devices, shifted(): return lax.ppermute(block, axis, route)  25.1 us
    dot_general x4, matrix products, shards(): jnp.einsum('rik,rkj->rij', left_all[step], right, precision=lax.Precision...  19.5 us
    unnamed x1, blocking collectives  15.4 us
    gather x4, local copies, waits for them, and re-layouts, shards(): right = rights[step][inner]  13.1 us
  transfers between devices with their start and end apart: 9, of which 5 were waited for; matrix products, arithmetic and copies ran while one was open for 5% of the time, Pallas kernels for 0%

commit v1 on v0

--- a/solution.py
+++ b/solution.py
@@ -1,9 +1,20 @@
+import functools
 import jax
 import jax.numpy as jnp
 from jax import lax
 from jax.sharding import PartitionSpec as P
 
 STEPS = 4
+
+
+def enter_arrays_over_axis(panel, device_axis):
+    return jnp.concatenate(
+        jax.lax.all_to_all(jnp.stack([panel] * jax.lax.axis_size(device_axis)), device_axis, 0, 0),
+        axis=1,
+    )
+
+
+_deliver_surface = functools.partial(enter_arrays_over_axis, device_axis="col")
 
 
 def shifted(block, axis, distance):
@@ -24,7 +35,7 @@
     bs = stored_blocks.shape[-1]
     row_index = lax.axis_index("row")
     col_index = lax.axis_index("col")
-    row_cols = lax.all_gather(block_cols, "col", axis=1, tiled=True)
+    row_cols = _deliver_surface(block_cols)
     col_cols = lax.all_gather(block_cols, "row", axis=0, tiled=True)[:, 0]
     held = stored_blocks[:, 0] * storage_map.astype(jnp.float32)[:, :, None]
     arrived = transposed(held, rows, cols)

time: 503 us -> 496 us (0.986)
  blocking collectives: 57.5 us -> 34.6 us
  starting transfers between devices: 37.3 us -> 49.7 us
    all_gather x1 -> x0, blocking collectives: 42.1 us -> none  [shards(): row_cols = lax.all_gather(block_cols, 'col', axis=1, tiled=True)]
    unnamed x1, blocking collectives: 15.4 us -> 34.6 us
    all_to_all x0 -> x1, starting transfers between devices: none -> 12.4 us  [enter_arrays_over_axis(): jax.lax.all_to_all(jnp.stack([panel] * jax.lax.axis_size(device_axis)), d...]
  transfers between devices with their start and end apart: 9 -> 10, of which waited for: 5 -> 5; matrix products, arithmetic and copies ran while one was open for 5% -> 6% of each run, Pallas kernels for 0% -> 0%
where the time goes in v1:
time: 496 us; the launch traced here: 491 us
  waiting for transfers between devices  322 us (65%)
  starting transfers between devices  49.7 us (10%)
  local copies, waits for them, and re-layouts  38.6 us (8%)
  blocking collectives  34.6 us (7%)
  matrix products  19.5 us (4%)
  between operations  14.4 us (3%)
  other arithmetic  12.3 us (2%)
    ppermute x1, waiting for transfers between devices, transposed(): return lax.ppermute(block, ('row', 'col'), route)  159 us
    all_to_all x1, waiting for transfers between devices, shards(): spread = lax.all_to_all(pieces, 'col', 1, 1, tiled=True)  96.6 us
    ppermute x6, waiting for transfers between devices, shifted(): return lax.ppermute(block, axis, route)  66.8 us
    unnamed x1, blocking collectives  34.6 us
    ppermute x6, starting transfers between devices, shifted(): return lax.ppermute(block, axis, route)  25.1 us
    dot_general x4, matrix products, shards(): jnp.einsum('rik,rkj->rij', left_all[step], right, precision=lax.Precision...  19.5 us
    gather x4, local copies, waits for them, and re-layouts, shards(): right = rights[step][inner]  13.1 us
    all_to_all x1, starting transfers between devices, enter_arrays_over_axis(): jax.lax.all_to_all(jnp.stack([panel] * jax.lax.axis_size(device_axis)), d...  12.4 us
  transfers between devices with their start and end apart: 10, of which 5 were waited for; matrix products, arithmetic and copies ran while one was open for 6% of the time, Pallas kernels for 0%

profile of v1, /device:TPU:2, one launch (start us, length us, event | category | flops | bytes accessed | tf_op | source)
XLA Modules:
  0.0 491.2 jit_solution(16983076751220349429)
XLA Ops:
  6.5 0.7 convert_bitcast_fusion
  7.2 0.7 convert_reduce_fusion
  7.9 0.0 copy-start.5
  7.9 1.9 copy.13
  9.8 0.0 copy-done.5
  9.8 0.7 scatter_custom_fusion
  10.5 0.1 mul.37
  10.6 1.5 bitcast_multiply_fusion
  12.2 3.6 gather_fusion.1
  15.8 0.0 copy-start.3
  15.8 1.9 broadcast_multiply_fusion
  17.7 0.3 copy-done.3
  18.0 2.2 pad_maximum_fusion
  20.2 10.2 %all-to-all-start.1 = ((f32[2,16,2,128,128]{4,3,2,0,1:T(8,128)}), f32[2,16,2,128,128]{4,3,2,0,1:T(8,128)}, u32[]{:S(2)}, u32[]{:S(2)}) async-start(f32[2,16,2,128,128]{4,3,2,0,1:T(8,128)} %pad_maximum_fusion), calls=%async_computation.1 | async-start | bytes 8388608 | tf_op jit(solution)/shard_map/all_to_all | solution.py:51
  30.4 0.0 all-gather.3.cloned.1.call-start
  30.6 96.6 %all-to-all-done.1 = f32[2,16,2,128,128]{4,3,2,0,1:T(8,128)} async-done(((f32[2,16,2,128,128]{4,3,2,0,1:T(8,128)}), f32[2,16,2,128,128]{4,3,2,0,1:T(8,128)}, u32[]{:S(2)}, u32[]{:S(2)}) %all-to-all-start.1) | async-done | bytes 4194336 | tf_op jit(solution)/shard_map/all_to_all | solution.py:51
  127.1 2.5 fusion.15
  129.6 0.0 copy-start.4
  129.6 1.3 copy-done.4
  131.0 0.2 collective-permute-start
  131.3 3.0 collective-permute-start.1
  134.3 1.1 collective-permute-start.2
  135.4 0.0 collective-permute-done
  135.4 5.2 %collective-permute-done.1 = f32[2,128,128]{2,1,0:T(8,128)S(1)} collective-permute-done((f32[2,128,128]{2,1,0:T(8,128)S(1)}, f32[2,128,128]{2,1,0:T(8,128)S(1)}, u32[]{:S(2)}, u32[]{:S(2)}) %collective-permute-start.1) | collective-permute-done | bytes 131104 | tf_op jit(solution)/shard_map/ppermute | solution.py:23
  140.6 1.3 collective-permute-done.2
  141.8 1.1 fusion.2
  142.9 0.8 pad_maximum_fusion.1
  143.8 0.0 all-gather.3.cloned.1.call-update
  143.8 1.9 collective-permute-start.3
  145.7 158.7 %collective-permute-done.3 = f32[32,128,128]{1,2,0:T(8,128)} collective-permute-done((f32[32,128,128]{1,2,0:T(8,128)}, f32[32,128,128]{1,2,0:T(8,128)}, u32[]{:S(2)}, u32[]{:S(2)}) %collective-permute-start.3) | collective-permute-done | bytes 2097184 | tf_op jit(solution)/shard_map/ppermute | solution.py:28
  304.5 3.1 copy.15
  307.5 3.7 gather_fusion.2
  311.2 3.2 bitcast_add_fusion
  314.4 0.0 collective-permute-start.5
  314.4 6.1 %collective-permute-start.4 = (f32[32,128,128]{1,2,0:T(8,128)}, f32[32,128,128]{1,2,0:T(8,128)}, u32[]{:S(2)}, u32[]{:S(2)}) collective-permute-start(f32[32,128,128]{1,2,0:T(8,128)} %bitcast_add_fusion), channel_id=1, source_target_pairs={{16,0},{32,16},{48,32},{64,48},{80,64},{96,80},{112,96},{128,112},... | collective-permute-start | bytes 6291464 | tf_op jit(solution)/shard_map/ppermute | solution.py:23
  320.4 60.3 %collective-permute-done.5 = f32[32,128,128]{1,2,0:T(8,128)} collective-permute-done((f32[32,128,128]{1,2,0:T(8,128)}, f32[32,128,128]{1,2,0:T(8,128)}, u32[]{:S(2)}, u32[]{:S(2)}) %collective-permute-start.5) | collective-permute-done | bytes 2097184 | tf_op jit(solution)/shard_map/ppermute | solution.py:23
  380.8 14.7 %collective-permute-start.6 = (f32[32,128,128]{1,2,0:T(8,128)}, f32[32,128,128]{1,2,0:T(8,128)}, u32[]{:S(2)}, u32[]{:S(2)}) collective-permute-start(f32[32,128,128]{1,2,0:T(8,128)} %collective-permute-done.5), channel_id=1, source_target_pairs={{16,0},{32,16},{48,32},{64,48},{80,64},{96,80},{112,96},{128,112},... | collective-permute-start | bytes 6291464 | tf_op jit(solution)/shard_map/ppermute | solution.py:23
  395.4 0.6 stack.14
  396.0 12.4 %all-to-all-start = ((s32[16,32,1]{1,2,0:T(1,128)}), s32[16,32,1]{1,2,0:T(1,128)S(1)}, u32[]{:S(2)}, u32[]{:S(2)}) async-start(s32[16,32,1]{1,2,0:T(1,128)} %stack.14), calls=%async_computation | async-start | bytes 16384 | tf_op jit(solution)/shard_map/all_to_all | solution.py:12
  408.5 0.0 copy-done.6
  408.5 0.6 dynamic-slice.32
  409.8 0.1 bitcast_dynamic-update-slice_fusion
  409.9 34.6 %all-reduce = s32[512]{0:T(512)S(1)} all-reduce(s32[512]{0:T(512)S(1)} %bitcast_dynamic-update-slice_fusion), channel_id=1, replica_groups=mesh['row'=16,'col'=16] {'row'}, use_global_device_ids=true, to_apply=%add | all-reduce | flops 512 | bytes 4096
  444.5 0.1 fusion.16
  444.6 0.0 all-to-all-done
  444.6 0.7 gather_fusion
  445.3 0.7 gather_fusion.4
  446.0 0.7 gather_fusion.6
  446.7 0.7 gather_fusion.8
  447.4 3.6 gather_fusion.3
  451.0 2.3 gather_fusion.7
  453.3 0.0 collective-permute-done.4
  453.3 3.6 gather_fusion.5
  456.9 0.0 collective-permute-done.6
  456.9 3.7 gather_fusion.9
  460.6 4.2 fusion.14
  464.7 0.0 copy-done.1
  464.8 0.0 copy-start
  464.8 4.5 fusion.18
  469.3 0.0 copy-done
  469.3 4.5 fusion.17
  473.8 4.5 fusion.19
  478.3 0.0 copy-done.2
  478.3 6.0 %add_bitcast_fusion = f32[32,1,128,128]{3,2,1,0:T(8,128)} fusion(f32[32,128,128]{2,1,0:T(8,128)S(1)} %fusion.19, f32[32,128,128]{2,1,0:T(8,128)S(1)} %fusion.18, f32[32,128,128]{2,1,0:T(8,128)S(1)} %fusion.17, f32[32,128,128]{2,1,0:T(8,128)S(1)} %bitcast.98, f32[32,128,128]{1,2,0:T(8,128)S(1)} %copy-done.2, pred[32]{0:T(512)(128)(4,1)S(1)} %get-tuple-element.29, ...), kind=kOutput, calls=%fused_computation.14 | convolution fusion | flops 808976384 | bytes 12583040 | tf_op jit(solution)/shard_map/rik,rkj->rij/dot_general | solution.py:74
  (17 shorter events, 0.1 us)
Async XLA Ops:
  7.9 1.9 copy-start.5
  15.8 2.2 copy-start.3
  20.2 106.9 %all-to-all-start.1 = ((f32[2,16,2,128,128]{4,3,2,0,1:T(8,128)}), f32[2,16,2,128,128]{4,3,2,0,1:T(8,128)}, u32[]{:S(2)}, u32[]{:S(2)}) async-start(f32[2,16,2,128,128]{4,3,2,0,1:T(8,128)} %pad_maximum_fusion), calls=%async_computation.1 | async-start | bytes 8388608 | tf_op jit(solution)/shard_map/all_to_all | solution.py:51
  30.4 430.1 %all-gather.3.cloned.1.call-start = ((), (), s32[]{:S(2)}) async-start(), calls=%async_computation.2 | async-start | bytes 8912896 | tf_op jit(solution)/shard_map/all_gather | solution.py:60
  129.6 1.3 copy-start.4
  131.0 4.4 collective-permute-start
  131.3 9.3 %collective-permute-start.1 = (f32[2,128,128]{2,1,0:T(8,128)S(1)}, f32[2,128,128]{2,1,0:T(8,128)S(1)}, u32[]{:S(2)}, u32[]{:S(2)}) collective-permute-start(f32[2,128,128]{2,1,0:T(8,128)S(1)} %get-tuple-element.13), channel_id=1, source_target_pairs={{32,0},{48,16},{64,32},{80,48},{96,64},{112,80},{128,96},{144,112}... | collective-permute-start | bytes 393224 | tf_op jit(solution)/shard_map/ppermute | solution.py:23
  134.3 7.5 %collective-permute-start.2 = (f32[2,128,128]{2,1,0:T(8,128)S(1)}, f32[2,128,128]{2,1,0:T(8,128)S(1)}, u32[]{:S(2)}, u32[]{:S(2)}) collective-permute-start(f32[2,128,128]{2,1,0:T(8,128)S(1)} %get-tuple-element.12), channel_id=1, source_target_pairs={{48,0},{64,16},{80,32},{96,48},{112,64},{128,80},{144,96},{160,112... | collective-permute-start | bytes 393224 | tf_op jit(solution)/shard_map/ppermute | solution.py:23
  143.8 160.7 %collective-permute-start.3 = (f32[32,128,128]{1,2,0:T(8,128)}, f32[32,128,128]{1,2,0:T(8,128)}, u32[]{:S(2)}, u32[]{:S(2)}) collective-permute-start(f32[32,128,128]{1,2,0:T(8,128)} %bitcast_multiply_fusion), channel_id=1, source_target_pairs={{0,0},{16,1},{32,2},{48,3},{64,4},{80,5},{96,6},{112,7},{128,8},{1... | collective-permute-start | bytes 6291464 | tf_op jit(solution)/shard_map/ppermute | solution.py:28
  311.2 97.3 %copy-start.6 = (u32[256]{0:T(256)S(1)}, u32[256]{0:T(256)}, u32[]{:S(2)}) copy-start(u32[256]{0:T(256)} %constant.122) | copy-start | bytes 3076
  314.4 66.4 %collective-permute-start.5 = (f32[32,128,128]{1,2,0:T(8,128)}, f32[32,128,128]{1,2,0:T(8,128)}, u32[]{:S(2)}, u32[]{:S(2)}) collective-permute-start(f32[32,128,128]{1,2,0:T(8,128)} %bitcast_add_fusion), channel_id=1, source_target_pairs={{32,0},{48,16},{64,32},{80,48},{96,64},{112,80},{128,96},{144,112}... | collective-permute-start | bytes 6291464 | tf_op jit(solution)/shard_map/ppermute | solution.py:23
  314.4 138.9 %collective-permute-start.4 = (f32[32,128,128]{1,2,0:T(8,128)}, f32[32,128,128]{1,2,0:T(8,128)}, u32[]{:S(2)}, u32[]{:S(2)}) collective-permute-start(f32[32,128,128]{1,2,0:T(8,128)} %bitcast_add_fusion), channel_id=1, source_target_pairs={{16,0},{32,16},{48,32},{64,48},{80,64},{96,80},{112,96},{128,112},... | collective-permute-start | bytes 6291464 | tf_op jit(solution)/shard_map/ppermute | solution.py:23
  380.8 76.1 %collective-permute-start.6 = (f32[32,128,128]{1,2,0:T(8,128)}, f32[32,128,128]{1,2,0:T(8,128)}, u32[]{:S(2)}, u32[]{:S(2)}) collective-permute-start(f32[32,128,128]{1,2,0:T(8,128)} %collective-permute-done.5), channel_id=1, source_target_pairs={{16,0},{32,16},{48,32},{64,48},{80,64},{96,80},{112,96},{128,112},... | collective-permute-start | bytes 6291464 | tf_op jit(solution)/shard_map/ppermute | solution.py:23
  396.0 48.6 %all-to-all-start = ((s32[16,32,1]{1,2,0:T(1,128)}), s32[16,32,1]{1,2,0:T(1,128)S(1)}, u32[]{:S(2)}, u32[]{:S(2)}) async-start(s32[16,32,1]{1,2,0:T(1,128)} %stack.14), calls=%async_computation | async-start | bytes 16384 | tf_op jit(solution)/shard_map/all_to_all | solution.py:12
  460.5 4.2 copy-start.1
  464.8 4.5 copy-start
  473.8 4.5 copy-start.2
Sparse Core Ops, SparseCore 0:
  143.9 279.6 all-gather.2
